TPU v7x, 128 devices: a whole 4x4x4 slice. The times are simulated.
128 devices in a mesh: dp: 4 (over y_hi, core), head: 4 (over x), ctx: 8 (over z, y_lo).
Axes of the slice: x: 4, y: 4 (y_hi: 2, y_lo: 2; y = y_hi * 2 + y_lo), z: 4, core: 2. Of those that a mesh axis runs over, the one named last changes fastest.
Arguments:
- video: bfloat16 [16, 64, 24576], P('dp', 'head', 'ctx'), parts along dimension 0, may hold values from -6 to 6
- cache: bfloat16 [8, 64, 24576], P('dp', 'head', 'ctx'), parts along dimension 0, may hold values from -6 to 6
- conv_weight: bfloat16 [3, 3, 288, 192], replicated, may hold values from -0.125 to 0.125
- conv_bias: float32 [192], replicated, may hold values from -3 to 3
- down_weight: bfloat16 [768, 192], replicated, may hold values from -0.21875 to 0.21875
- patch_weight: bfloat16 [768, 5120], P(None, ('head', 'ctx')), may hold values from -0.21875 to 0.21875
- step_index: int32 [4], P('dp'), parts along dimension 0, may hold values from 0 to 999
- mod_weight: bfloat16 [256, 10240], P(None, ('head', 'ctx')), may hold values from -1 to 1
- qkv_weight: bfloat16 [5120, 20, 3, 128], P('ctx', 'head'), may hold values from -0.078125 to 0.078125
Outputs:
- attended: bfloat16 [16384, 2560], P(('dp', 'ctx'), 'head'), parts along dimension 0
There are 4 independent parts, one for each index of `dp`. A program takes and returns all parts, laid end to end along the dimension named above; an argument that names none is the same for every part. Nothing has to cross between parts.
All inputs are finite; a program needn't handle non-finite values.
Results may differ from a plain program's by a relative error of at most 0.015.
The roundings to bfloat16 on the way count: a program that leaves them out, or rounds other values in their place, can miss the bound.
Values may be sent and summed in bfloat16 or wider, within the bound.
No kernel may reach another device: no remote copies, remote signals or barrier semaphores. Data moves between devices by JAX's collectives and lax.ppermute only.
A program may use at most 128 MiB of HBM per device.

v0:
```python
import jax
import jax.numpy as jnp
from jax import lax
from jax.sharding import PartitionSpec as P

D = 5120
HDIM = 128
FREQ = 256


def with_halo(cells, sides, width):
    for axis, dim in sides:
        count = lax.axis_size(axis)
        ends = count - 1
        head = lax.slice_in_dim(cells, 0, width, axis=dim)
        tail = lax.slice_in_dim(cells, cells.shape[dim] - width, cells.shape[dim], axis=dim)
        cells = jnp.concatenate(
            [
                lax.ppermute(tail, axis, [(i, (i + 1) % count) for i in range(ends)]),
                cells,
                lax.ppermute(head, axis, [((i + 1) % count, i) for i in range(ends)]),
            ],
            axis=dim,
        )
    return cells


def silu_act(value):
    return value * jax.nn.sigmoid(value)


def shards(
    video,
    cache,
    conv_weight,
    conv_bias,
    down_weight,
    patch_weight,
    step_index,
    mod_weight,
    qkv_weight,
):
    cin = conv_weight.shape[2] // 3
    cmid = conv_weight.shape[3]
    frame_count = video.shape[0]
    tile_rows = video.shape[1]
    tile_cols = video.shape[2] // cin
    frames = jnp.concatenate([cache, video], 0).reshape(frame_count + 2, tile_rows, tile_cols, cin)
    padded = with_halo(frames, (("head", 1), ("ctx", 2)), 1)
    total = jnp.zeros((frame_count, tile_rows, tile_cols, cmid), jnp.float32)
    for time_tap in range(3):
        for row_tap in range(3):
            slab = padded[time_tap : time_tap + frame_count, row_tap : row_tap + tile_rows]
            stacked = jnp.concatenate(
                [slab[:, :, col_tap : col_tap + tile_cols] for col_tap in range(3)], -1
            )
            total = total + jnp.einsum(
                "fyxc,cd->fyxd",
                stacked,
                conv_weight[time_tap, row_tap],
                preferred_element_type=jnp.float32,
            )
    hidden = silu_act(total + conv_bias).astype(jnp.bfloat16)
    stacked = (
        hidden.reshape(frame_count, tile_rows // 2, 2, tile_cols // 2, 2, cmid)
        .transpose(0, 1, 3, 2, 4, 5)
        .reshape(-1, 4 * cmid)
    )
    reduced = silu_act(jnp.dot(stacked, down_weight, preferred_element_type=jnp.float32)).astype(
        jnp.bfloat16
    )
    reduced = reduced.reshape(frame_count, tile_rows // 2, tile_cols // 2, cmid)
    patches = reduced.reshape(frame_count, tile_rows // 4, 2, tile_cols // 4, 2, cmid).transpose(
        0, 1, 3, 2, 4, 5
    )
    patches = patches.reshape(-1, 4 * cmid)
    half = FREQ // 2
    freqs = jnp.exp(-jnp.log(10000.0) * jnp.arange(half, dtype=jnp.float32) / half)
    angles = step_index[0].astype(jnp.float32) * freqs
    timing = jnp.concatenate([jnp.cos(angles), jnp.sin(angles)]).astype(jnp.bfloat16)
    mod_share = jnp.dot(timing[None, :], mod_weight, preferred_element_type=jnp.float32)[0]
    modulation = lax.all_gather(mod_share, ("head", "ctx"), axis=0, tiled=True)
    scale = modulation[:D]
    shift = modulation[D:]
    embedded = jnp.dot(
        patches,
        lax.all_gather(patch_weight, ("head", "ctx"), axis=1, tiled=True),
        preferred_element_type=jnp.float32,
    )
    inverse = lax.rsqrt(jnp.mean(embedded * embedded, -1, keepdims=True) + 1e-06)
    normed = (embedded * inverse * (1.0 + scale) + shift).astype(jnp.bfloat16)
    gathered = lax.all_gather(normed, "head", axis=0, tiled=True)
    group_rows = gathered.shape[0]
    heads_here = qkv_weight.shape[1]
    out_cols = heads_here * 3 * HDIM
    piece = lax.all_gather(qkv_weight, "ctx", axis=0, tiled=True)
    qkv = jnp.dot(
        gathered, piece.reshape(piece.shape[0], out_cols), preferred_element_type=jnp.float32
    )
    qkv = qkv.astype(jnp.bfloat16).reshape(group_rows, heads_here, 3, HDIM)
    query = qkv[:, :, 0]
    keys = qkv[:, :, 1]
    values = qkv[:, :, 2]
    inv_root = 1.0 / jnp.sqrt(jnp.float32(HDIM))
    best = jnp.full((heads_here, group_rows), -1e30, jnp.float32)
    key_piece = lax.all_gather(keys, "ctx", axis=0, tiled=True)
    value_piece = lax.all_gather(values, "ctx", axis=0, tiled=True)
    scores = (
        jnp.einsum("qhd,khd->hqk", query, key_piece, preferred_element_type=jnp.float32) * inv_root
    )
    new_best = jnp.maximum(best, jnp.max(scores, -1))
    probs = jnp.exp(scores - new_best[..., None])
    denom = jnp.sum(probs, -1)
    accum = jnp.einsum(
        "hqk,khd->hqd", probs.astype(jnp.bfloat16), value_piece, preferred_element_type=jnp.float32
    )
    best, denom, accum = (new_best, denom, accum)
    result = (accum / denom[..., None]).astype(jnp.bfloat16)
    return result.transpose(1, 0, 2).reshape(group_rows, heads_here * HDIM)


def solution(mesh):
    return jax.shard_map(
        shards,
        mesh=mesh,
        in_specs=(
            P("dp", "head", "ctx"),
            P("dp", "head", "ctx"),
            P(),
            P(),
            P(),
            P(None, ("head", "ctx")),
            P("dp"),
            P(None, ("head", "ctx")),
            P("ctx", "head", None, None),
        ),
        out_specs=P(("dp", "ctx"), "head"),
        check_vma=False,
    )
```

profile of v0, /device:TPU:1, one launch (start us, length us, event | category | flops | bytes accessed | tf_op | source)
XLA Modules:
  0.0 923.7 jit_solution(17581543572212077937)
XLA Ops:
  10.8 4.6 collective-permute-start
  15.3 1.3 collective-permute-start.1
  19.2 141.1 %all-reduce = f32[10240]{0:T(1024)S(1)} all-reduce(f32[10240]{0:T(1024)S(1)} %dynamic-update-slice), channel_id=1, replica_groups=mesh['dp'=4,'head'=4,'ctx'=8] {'head','ctx'}, use_global_device_ids=true, to_apply=%add | all-reduce | flops 10240 | bytes 81920
  164.3 1.3 collective-permute-start.2
  165.6 1.5 collective-permute-start.3
  167.6 1.4 collective-permute-done.2
  168.9 1.9 fusion.81
  170.8 1.3 collective-permute-done.3
  172.1 2.1 fusion.73
  181.5 2.6 multiply_convert_fusion
  187.7 8.9 all-gather.8.cloned.1.call-done
  196.7 5.9 multiply_reduce_fusion.1
  202.6 1.5 add_convert_fusion
  204.8 3.1 copy.17
  208.0 63.2 %all-gather.10.cloned.1.call-done = bf16[512,5120]{1,0:T(8,128)(2,1)} async-done(((bf16[128,5120]{1,0:T(8,128)(2,1)}), bf16[512,5120]{1,0:T(8,128)(2,1)}) %all-gather.10.cloned.1.call-update) | async-done | bytes 5242896 | tf_op jit(solution)/shard_map/all_gather | solution.py:92
  271.2 381.9 %all-gather.12.cloned.1.call-done = bf16[5120,5,3,128]{0,3,2,1:T(8,128)(2,1)} async-done(((bf16[640,5,3,128]{0,3,2,1:T(8,128)(2,1)}), bf16[5120,5,3,128]{0,3,2,1:T(8,128)(2,1)}) %all-gather.12.cloned.1.call-update) | async-done | bytes 19660816 | tf_op jit(solution)/shard_map/all_gather | solution.py:96
  653.1 17.7 %convolution_convert_fusion = bf16[512,1920]{1,0:T(8,128)(2,1)} fusion(bf16[512,5120]{1,0:T(8,128)(2,1)} %all-gather.10.cloned.1.call-done, bf16[5120,1920]{0,1:T(8,128)(2,1)} %bitcast.113), kind=kOutput, calls=%fused_computation.24 | convolution fusion | flops 10067312640 | bytes 26869760 | tf_op jit(solution)/shard_map/dot_general | solution.py:97
  670.8 2.7 copy.18
  674.5 1.1 copy.33
  676.2 110.6 %all-gather.14.cloned.1.call-done = bf16[4096,5,1,128]{3,0,1,2:T(8,128)(2,1)} async-done(((bf16[512,5,1,128]{3,0,1,2:T(8,128)(2,1)}), bf16[4096,5,1,128]{3,0,1,2:T(8,128)(2,1)}) %all-gather.14.cloned.1.call-update) | async-done | bytes 5242896 | tf_op jit(solution)/shard_map/all_gather | solution.py:106
  786.8 19.0 %multiply_reduce_fusion = (f32[5,512]{1,0:T(8,128)S(1)}, f32[5,512,4096]{2,1,0:T(8,128)}) fusion(bf16[4096,5,1,128]{3,0,1,2:T(8,128)(2,1)} %all-gather.14.cloned.1.call-done, bf16[512,5,3,128]{0,3,2,1:T(8,128)(2,1)S(1)} %bitcast.108), kind=kOutput, calls=%fused_computation.1 | convolution fusion | flops 2705323520 | bytes 47851520 | tf_op jit(solution)/shard_map/qhd,khd->hqk/dot_general | solution.py:109
  805.8 17.3 %fusion = f32[5,512]{1,0:T(8,128)S(1)} fusion(f32[5,512,4096]{2,1,0:T(8,128)} %get-tuple-element.47, f32[5,512]{1,0:T(8,128)S(1)} %broadcast_maximum_fusion), kind=kLoop, calls=%fused_computation.2 | loop fusion | flops 31454720 | bytes 41963520 | tf_op jit(solution)/shard_map/reduce_sum | solution.py:113
  823.2 75.6 %all-gather.16.cloned.1.call-done = bf16[4096,5,1,128]{0,3,1,2:T(8,128)(2,1)} async-done(((bf16[512,5,1,128]{0,3,1,2:T(8,128)(2,1)}), bf16[4096,5,1,128]{0,3,1,2:T(8,128)(2,1)}) %all-gather.16.cloned.1.call-update) | async-done | bytes 5242896 | tf_op jit(solution)/shard_map/all_gather | solution.py:107
  898.7 17.3 %divide_convert_fusion = bf16[512,5,128]{0,2,1:T(8,128)(2,1)S(1)} fusion(bf16[4096,5,1,128]{0,3,1,2:T(8,128)(2,1)} %all-gather.16.cloned.1.call-done, f32[5,512,4096]{2,1,0:T(8,128)} %get-tuple-element.47, f32[5,512]{1,0:T(8,128)S(1)} %broadcast_maximum_fusion, f32[512,5]{0,1:T(8,128)S(1)} %bitcast.112), kind=kOutput, calls=%fused_computation.84 | convolution fusion | flops 2716467200 | bytes 47861760 | tf_op jit(solution)/shard_map/hqk,khd->hqd/dot_general | solution.py:114
  (70 shorter events, 23.9 us)
Async XLA Ops:
  6.5 180.0 %copy-start = (bf16[768,192]{0,1:T(8,128)(2,1)S(1)}, bf16[768,192]{0,1:T(8,128)(2,1)}, u32[]{:S(2)}) copy-start(bf16[768,192]{0,1:T(8,128)(2,1)} %param.13) | copy-start | bytes 884740
  6.5 10.8 %copy-start.7 = (u32[128]{0:T(128)S(1)}, u32[128]{0:T(128)}, u32[]{:S(2)}) copy-start(u32[128]{0:T(128)} %constant.27) | copy-start | bytes 1540
  6.5 12.2 %copy-start.4 = (bf16[256,320]{0,1:T(8,128)(2,1)S(1)}, bf16[256,320]{0,1:T(8,128)(2,1)}, u32[]{:S(2)}) copy-start(bf16[256,320]{0,1:T(8,128)(2,1)} %param.16) | copy-start | bytes 491524
  6.5 190.1 %all-gather.8.cloned.1.call-start = ((), (), s32[]{:S(2)}) async-start(), calls=%async_computation | async-start | bytes 8110080 | tf_op jit(solution)/shard_map/all_gather | solution.py:87
  7.3 264.0 %all-gather.10.cloned.1.call-start = ((), (), s32[]{:S(2)}) async-start(), calls=%async_computation.1 | async-start | bytes 6553600 | tf_op jit(solution)/shard_map/all_gather | solution.py:92
  8.3 152.2 %copy-start.3 = (bf16[4,16,3072]{2,1,0:T(8,128)(2,1)S(1)}, bf16[4,16,3072]{2,1,0:T(8,128)(2,1)}, u32[]{:S(2)}) copy-start(bf16[4,16,3072]{2,1,0:T(8,128)(2,1)} %param.9) | copy-start | bytes 1179652
  10.8 151.3 %collective-permute-start = (bf16[6,1,32,96]{3,2,1,0:T(8,128)(2,1)}, bf16[6,1,32,96]{3,2,1,0:T(8,128)(2,1)}, u32[]{:S(2)}, u32[]{:S(2)}) collective-permute-start(bf16[6,1,32,96]{3,2,1,0:T(8,128)(2,1)} %get-tuple-element.35), channel_id=1, source_target_pairs={{0,8},{8,16},{16,24},{1,9},{9,17},{17,25},{2,10},{10,18},{18,26},{... | collective-permute-start | bytes 110600 | tf_op jit(solution)/shard_map/ppermute | solution.py:19
  15.3 148.0 %collective-permute-start.1 = (bf16[6,1,32,96]{3,2,1,0:T(8,128)(2,1)}, bf16[6,1,32,96]{3,2,1,0:T(8,128)(2,1)}, u32[]{:S(2)}, u32[]{:S(2)}) collective-permute-start(bf16[6,1,32,96]{3,2,1,0:T(8,128)(2,1)} %get-tuple-element.34), channel_id=1, source_target_pairs={{8,0},{16,8},{24,16},{9,1},{17,9},{25,17},{10,2},{18,10},{26,18},{... | collective-permute-start | bytes 110600 | tf_op jit(solution)/shard_map/ppermute | solution.py:21
  164.3 4.6 collective-permute-start.2
  165.6 6.5 collective-permute-start.3
  170.8 3.4 copy-start.5
  180.5 0.9 copy-start.6
  202.6 2.2 copy-start.2
  204.1 449.0 %all-gather.12.cloned.1.call-start = ((), (), s32[]{:S(2)}) async-start(), calls=%async_computation.2 | async-start | bytes 22118400 | tf_op jit(solution)/shard_map/all_gather | solution.py:96
  207.9 578.8 %all-gather.14.cloned.1.call-start = ((), (), s32[]{:S(2)}) async-start(), calls=%async_computation.3 | async-start | bytes 5898240 | tf_op jit(solution)/shard_map/all_gather | solution.py:106
  675.6 223.2 %all-gather.16.cloned.1.call-start = ((), (), s32[]{:S(2)}) async-start(), calls=%async_computation.4 | async-start | bytes 5898240 | tf_op jit(solution)/shard_map/all_gather | solution.py:107
  898.7 18.4 %copy-start.1 = (bf16[768,192]{0,1:T(8,128)(2,1)S(1)}, bf16[768,192]{0,1:T(8,128)(2,1)}, u32[]{:S(2)}) copy-start(bf16[768,192]{0,1:T(8,128)(2,1)} %param.13) | copy-start | bytes 884740
Sparse Core Ops, SparseCore 0:
  9.0 187.6 all-gather.7
  204.2 66.9 all-gather.9
  272.9 380.1 all-gather.11
  675.7 111.0 all-gather.13
  788.3 110.4 all-gather.15
where the time goes:
time: 924 us
  waiting for transfers between devices  644 us (70%)
  blocking collectives  141 us (15%)
  matrix products  70.4 us (8%)
  other arithmetic  22.9 us (2%)
  local copies, waits for them, and re-layouts  21.4 us (2%)
  between operations  14.9 us (2%)
    all_gather x1, waiting for transfers between devices, shards(): piece = lax.all_gather(qkv_weight, 'ctx', axis=0, tiled=True)  382 us
    unnamed x1, blocking collectives  141 us
    all_gather x1, waiting for transfers between devices, shards(): key_piece = lax.all_gather(keys, 'ctx', axis=0, tiled=True)  111 us
    all_gather x1, waiting for transfers between devices, shards(): value_piece = lax.all_gather(values, 'ctx', axis=0, tiled=True)  75.6 us
    all_gather x1, waiting for transfers between devices, shards(): gathered = lax.all_gather(normed, 'head', axis=0, tiled=True)  63.2 us
    dot_general x1, matrix products, shards(): jnp.einsum('qhd,khd->hqk', query, key_piece, preferred_element_type=jnp.f...  19 us
  transfers between devices with their start and end apart: 9, of which 7 were waited for; matrix products, arithmetic and copies ran while one was open for 7% of the time, Pallas kernels for 0%

commit v1 on v0

--- a/solution.py
+++ b/solution.py
@@ -89,7 +89,12 @@
     )
     inverse = lax.rsqrt(jnp.mean(embedded * embedded, -1, keepdims=True) + 1e-06)
     normed = (embedded * inverse * (1.0 + scale) + shift).astype(jnp.bfloat16)
-    gathered = lax.all_gather(normed, "head", axis=0, tiled=True)
+    ring = [normed]
+    for hop in range(3):
+        ring.append(lax.ppermute(ring[-1], "head", [(dev, (dev + 1) % 4) for dev in range(4)]))
+    gathered = jnp.roll(
+        jnp.concatenate(ring[::-1], axis=0), (lax.axis_index("head") + 1) * ring[0].shape[0], axis=0
+    )
     group_rows = gathered.shape[0]
     heads_here = qkv_weight.shape[1]
     out_cols = heads_here * 3 * HDIM

time: 924 us -> 850 us (0.920)
  waiting for transfers between devices: 644 us -> 547 us
  local copies, waits for them, and re-layouts: 21.4 us -> 35.1 us
  starting transfers between devices: 8.77 us -> 19.2 us
    all_gather x1, waiting for transfers between devices: 382 us -> 282 us  [shards(): piece = lax.all_gather(qkv_weight, 'ctx', axis=0, tiled=True)]
    ppermute x0 -> x3, waiting for transfers between devices: none -> 67.1 us  [shards(): lax.ppermute(ring[-1], 'head', [(dev, (dev + 1) % 4) for dev in range(4)])]
    all_gather x1 -> x0, waiting for transfers between devices: 63.2 us -> none  [shards(): gathered = lax.all_gather(normed, 'head', axis=0, tiled=True)]
    unnamed x24 -> x34, local copies, waits for them, and re-layouts: 8.06 us -> 22.8 us
    ppermute x0 -> x3, starting transfers between devices: none -> 10.5 us  [shards(): lax.ppermute(ring[-1], 'head', [(dev, (dev + 1) % 4) for dev in range(4)])]
  transfers between devices with their start and end apart: 9 -> 11, of which waited for: 7 -> 9; matrix products, arithmetic and copies ran while one was open for 7% -> 10% of each run, Pallas kernels for 0% -> 0%
where the time goes in v1:
time: 850 us; the launch traced here: 849 us
  waiting for transfers between devices  547 us (64%)
  blocking collectives  138 us (16%)
  matrix products  70.4 us (8%)
  local copies, waits for them, and re-layouts  35.1 us (4%)
  other arithmetic  24.9 us (3%)
  starting transfers between devices  19.2 us (2%)
  between operations  14.8 us (2%)
    all_gather x1, waiting for transfers between devices, shards(): piece = lax.all_gather(qkv_weight, 'ctx', axis=0, tiled=True)  282 us
    unnamed x1, blocking collectives  138 us
    all_gather x1, waiting for transfers between devices, shards(): key_piece = lax.all_gather(keys, 'ctx', axis=0, tiled=True)  111 us
    all_gather x1, waiting for transfers between devices, shards(): value_piece = lax.all_gather(values, 'ctx', axis=0, tiled=True)  75.6 us
    ppermute x3, waiting for transfers between devices, shards(): lax.ppermute(ring[-1], 'head', [(dev, (dev + 1) % 4) for dev in range(4)])  67.1 us
    unnamed x34, local copies, waits for them, and re-layouts  22.8 us
    dot_general x1, matrix products, shards(): jnp.einsum('qhd,khd->hqk', query, key_piece, preferred_element_type=jnp.f...  19.1 us
    dot_general x1, matrix products, shards(): jnp.dot(gathered, piece.reshape(piece.shape[0], out_cols), preferred_elem...  17.7 us
  transfers between devices with their start and end apart: 11, of which 9 were waited for; matrix products, arithmetic and copies ran while one was open for 10% of the time, Pallas kernels for 0%

profile of v1, /device:TPU:1, one launch (start us, length us, event | category | flops | bytes accessed | tf_op | source)
XLA Modules:
  0.0 849.1 jit_solution(3823362946533361527)
XLA Ops:
  7.3 5.1 copy.17
  14.9 4.6 collective-permute-start
  23.2 138.2 %all-reduce = f32[10240]{0:T(1024)S(1)} all-reduce(f32[10240]{0:T(1024)S(1)} %dynamic-update-slice), channel_id=1, replica_groups=mesh['dp'=4,'head'=4,'ctx'=8] {'head','ctx'}, use_global_device_ids=true, to_apply=%add | all-reduce | flops 10240 | bytes 81920
  170.0 1.9 fusion.86
  173.2 2.1 fusion.78
  182.6 2.6 multiply_convert_fusion
  188.8 7.1 all-gather.7.cloned.1.call-done
  195.9 5.9 multiply_reduce_fusion.1
  203.1 17.1 %collective-permute-done.4 = bf16[128,5120]{1,0:T(8,128)(2,1)S(1)} collective-permute-done((bf16[128,5120]{1,0:T(8,128)(2,1)S(1)}, bf16[128,5120]{1,0:T(8,128)(2,1)S(1)}, u32[]{:S(2)}, u32[]{:S(2)}) %collective-permute-start.4) | collective-permute-done | bytes 1310752 | tf_op jit(solution)/shard_map/ppermute | solution.py:94
  221.3 9.4 %collective-permute-start.5 = (bf16[128,5120]{1,0:T(8,128)(2,1)S(1)}, bf16[128,5120]{1,0:T(8,128)(2,1)}, u32[]{:S(2)}, u32[]{:S(2)}) collective-permute-start(bf16[128,5120]{1,0:T(8,128)(2,1)S(1)} %collective-permute-done.4), channel_id=1, source_target_pairs={{0,8},{8,16},{16,24},{24,0},{1,9},{9,17},{17,25},{25,1},{2,10},{10... | collective-permute-start | bytes 3932168 | tf_op jit(solution)/shard_map/ppermute | solution.py:94
  230.6 23.1 %collective-permute-done.5 = bf16[128,5120]{1,0:T(8,128)(2,1)} collective-permute-done((bf16[128,5120]{1,0:T(8,128)(2,1)S(1)}, bf16[128,5120]{1,0:T(8,128)(2,1)}, u32[]{:S(2)}, u32[]{:S(2)}) %collective-permute-start.5) | collective-permute-done | bytes 1310752 | tf_op jit(solution)/shard_map/ppermute | solution.py:94
  254.2 26.9 %collective-permute-done.6 = bf16[128,5120]{1,0:T(8,128)(2,1)} collective-permute-done((bf16[128,5120]{1,0:T(8,128)(2,1)}, bf16[128,5120]{1,0:T(8,128)(2,1)}, u32[]{:S(2)}, u32[]{:S(2)}) %collective-permute-start.6) | collective-permute-done | bytes 1310752 | tf_op jit(solution)/shard_map/ppermute | solution.py:94
  281.0 2.5 constant_dynamic-update-slice_fusion.16
  283.5 2.5 constant_dynamic-update-slice_fusion.15
  288.7 2.6 constant_dynamic-update-slice_fusion.12
  291.3 2.5 constant_dynamic-update-slice_fusion.11
  296.4 282.0 %all-gather.9.cloned.1.call-done = bf16[5120,5,3,128]{0,3,2,1:T(8,128)(2,1)} async-done(((bf16[640,5,3,128]{0,3,2,1:T(8,128)(2,1)}), bf16[5120,5,3,128]{0,3,2,1:T(8,128)(2,1)}) %all-gather.9.cloned.1.call-update) | async-done | bytes 19660816 | tf_op jit(solution)/shard_map/all_gather | solution.py:101
  578.5 17.7 %fusion.9 = bf16[512,1920]{1,0:T(8,128)(2,1)} fusion(bf16[5120,1920]{0,1:T(8,128)(2,1)} %bitcast.112, bf16[1024,5120]{1,0:T(8,128)(2,1)} %constant_dynamic-update-slice_fusion.9, s32[]{:T(128)S(6)} %select_n.14), kind=kOutput, calls=%fused_computation.26 | convolution fusion | flops 10067312640 | bytes 26869764 | tf_op jit(solution)/shard_map/dot_general | solution.py:102
  596.2 2.7 copy.18
  601.5 110.7 %all-gather.11.cloned.1.call-done = bf16[4096,5,1,128]{3,0,1,2:T(8,128)(2,1)} async-done(((bf16[512,5,1,128]{3,0,1,2:T(8,128)(2,1)}), bf16[4096,5,1,128]{3,0,1,2:T(8,128)(2,1)}) %all-gather.11.cloned.1.call-update) | async-done | bytes 5242896 | tf_op jit(solution)/shard_map/all_gather | solution.py:111
  712.2 19.1 %multiply_reduce_fusion = (f32[5,512]{1,0:T(8,128)S(1)}, f32[5,512,4096]{2,1,0:T(8,128)}) fusion(bf16[4096,5,1,128]{3,0,1,2:T(8,128)(2,1)} %all-gather.11.cloned.1.call-done, bf16[512,5,3,128]{0,3,2,1:T(8,128)(2,1)S(1)} %bitcast.107), kind=kOutput, calls=%fused_computation.1 | convolution fusion | flops 2705323520 | bytes 47851520 | tf_op jit(solution)/shard_map/qhd,khd->hqk/dot_general | solution.py:114
  731.3 17.3 %fusion = f32[5,512]{1,0:T(8,128)S(1)} fusion(f32[5,512,4096]{2,1,0:T(8,128)} %get-tuple-element.47, f32[5,512]{1,0:T(8,128)S(1)} %broadcast_maximum_fusion), kind=kLoop, calls=%fused_computation.2 | loop fusion | flops 31454720 | bytes 41963520 | tf_op jit(solution)/shard_map/reduce_sum | solution.py:118
  748.6 75.6 %all-gather.13.cloned.1.call-done = bf16[4096,5,1,128]{0,3,1,2:T(8,128)(2,1)} async-done(((bf16[512,5,1,128]{0,3,1,2:T(8,128)(2,1)}), bf16[4096,5,1,128]{0,3,1,2:T(8,128)(2,1)}) %all-gather.13.cloned.1.call-update) | async-done | bytes 5242896 | tf_op jit(solution)/shard_map/all_gather | solution.py:112
  824.2 17.3 %divide_convert_fusion = bf16[512,5,128]{0,2,1:T(8,128)(2,1)S(1)} fusion(bf16[4096,5,1,128]{0,3,1,2:T(8,128)(2,1)} %all-gather.13.cloned.1.call-done, f32[5,512,4096]{2,1,0:T(8,128)} %get-tuple-element.47, f32[5,512]{1,0:T(8,128)S(1)} %broadcast_maximum_fusion, f32[512,5]{0,1:T(8,128)S(1)} %bitcast.111), kind=kOutput, calls=%fused_computation.86 | convolution fusion | flops 2716467200 | bytes 47861760 | tf_op jit(solution)/shard_map/hqk,khd->hqd/dot_general | solution.py:119
  (85 shorter events, 37.9 us)
Async XLA Ops:
  6.5 181.1 %copy-start = (bf16[768,192]{0,1:T(8,128)(2,1)S(1)}, bf16[768,192]{0,1:T(8,128)(2,1)}, u32[]{:S(2)}) copy-start(bf16[768,192]{0,1:T(8,128)(2,1)} %param.13) | copy-start | bytes 884740
  6.5 189.4 %all-gather.7.cloned.1.call-start = ((), (), s32[]{:S(2)}) async-start(), calls=%async_computation | async-start | bytes 8110080 | tf_op jit(solution)/shard_map/all_gather | solution.py:87
  7.3 571.2 %all-gather.9.cloned.1.call-start = ((), (), s32[]{:S(2)}) async-start(), calls=%async_computation.1 | async-start | bytes 22118400 | tf_op jit(solution)/shard_map/all_gather | solution.py:101
  12.4 0.9 copy-start.5
  12.4 1.1 copy-start.4
  12.4 9.1 %copy-start.9 = (u32[128]{0:T(128)S(1)}, u32[128]{0:T(128)}, u32[]{:S(2)}) copy-start(u32[128]{0:T(128)} %constant.58) | copy-start | bytes 1540
  12.4 10.4 %copy-start.6 = (bf16[256,320]{0,1:T(8,128)(2,1)S(1)}, bf16[256,320]{0,1:T(8,128)(2,1)}, u32[]{:S(2)}) copy-start(bf16[256,320]{0,1:T(8,128)(2,1)} %param.16) | copy-start | bytes 491524
  12.4 699.8 %all-gather.11.cloned.1.call-start = ((), (), s32[]{:S(2)}) async-start(), calls=%async_computation.2 | async-start | bytes 5898240 | tf_op jit(solution)/shard_map/all_gather | solution.py:111
  14.9 148.2 %collective-permute-start = (bf16[6,1,32,96]{3,2,1,0:T(8,128)(2,1)}, bf16[6,1,32,96]{3,2,1,0:T(8,128)(2,1)}, u32[]{:S(2)}, u32[]{:S(2)}) collective-permute-start(bf16[6,1,32,96]{3,2,1,0:T(8,128)(2,1)} %get-tuple-element.35), channel_id=1, source_target_pairs={{0,8},{8,16},{16,24},{1,9},{9,17},{17,25},{2,10},{10,18},{18,26},{... | collective-permute-start | bytes 110600 | tf_op jit(solution)/shard_map/ppermute | solution.py:19
  19.5 145.0 %collective-permute-start.1 = (bf16[6,1,32,96]{3,2,1,0:T(8,128)(2,1)}, bf16[6,1,32,96]{3,2,1,0:T(8,128)(2,1)}, u32[]{:S(2)}, u32[]{:S(2)}) collective-permute-start(bf16[6,1,32,96]{3,2,1,0:T(8,128)(2,1)} %get-tuple-element.34), channel_id=1, source_target_pairs={{8,0},{16,8},{24,16},{9,1},{17,9},{25,17},{10,2},{18,10},{26,18},{... | collective-permute-start | bytes 110600 | tf_op jit(solution)/shard_map/ppermute | solution.py:21
  165.4 4.6 collective-permute-start.2
  166.7 6.5 collective-permute-start.3
  171.9 3.5 copy-start.7
  181.7 0.9 copy-start.8
  202.3 17.9 %collective-permute-start.4 = (bf16[128,5120]{1,0:T(8,128)(2,1)S(1)}, bf16[128,5120]{1,0:T(8,128)(2,1)S(1)}, u32[]{:S(2)}, u32[]{:S(2)}) collective-permute-start(bf16[128,5120]{1,0:T(8,128)(2,1)S(1)} %add_convert_fusion), channel_id=1, source_target_pairs={{0,8},{8,16},{16,24},{24,0},{1,9},{9,17},{17,25},{25,1},{2,10},{10... | collective-permute-start | bytes 3932168 | tf_op jit(solution)/shard_map/ppermute | solution.py:94
  220.2 1.1 copy-start.2
  221.3 32.5 %collective-permute-start.5 = (bf16[128,5120]{1,0:T(8,128)(2,1)S(1)}, bf16[128,5120]{1,0:T(8,128)(2,1)}, u32[]{:S(2)}, u32[]{:S(2)}) collective-permute-start(bf16[128,5120]{1,0:T(8,128)(2,1)S(1)} %collective-permute-done.4), channel_id=1, source_target_pairs={{0,8},{8,16},{16,24},{24,0},{1,9},{9,17},{17,25},{25,1},{2,10},{10... | collective-permute-start | bytes 3932168 | tf_op jit(solution)/shard_map/ppermute | solution.py:94
  253.8 27.2 %collective-permute-start.6 = (bf16[128,5120]{1,0:T(8,128)(2,1)}, bf16[128,5120]{1,0:T(8,128)(2,1)}, u32[]{:S(2)}, u32[]{:S(2)}) collective-permute-start(bf16[128,5120]{1,0:T(8,128)(2,1)} %collective-permute-done.5), channel_id=1, source_target_pairs={{0,8},{8,16},{16,24},{24,0},{1,9},{9,17},{17,25},{25,1},{2,10},{10... | collective-permute-start | bytes 3932168 | tf_op jit(solution)/shard_map/ppermute | solution.py:94
  254.2 31.9 %copy-start.3 = (bf16[128,5120]{1,0:T(8,128)(2,1)S(1)}, bf16[128,5120]{1,0:T(8,128)(2,1)}, u32[]{:S(2)}) copy-start(bf16[128,5120]{1,0:T(8,128)(2,1)} %copy-done.2) | copy-start | bytes 3932164
  600.9 223.3 %all-gather.13.cloned.1.call-start = ((), (), s32[]{:S(2)}) async-start(), calls=%async_computation.3 | async-start | bytes 5898240 | tf_op jit(solution)/shard_map/all_gather | solution.py:112
  824.2 18.4 %copy-start.1 = (bf16[768,192]{0,1:T(8,128)(2,1)S(1)}, bf16[768,192]{0,1:T(8,128)(2,1)}, u32[]{:S(2)}) copy-start(bf16[768,192]{0,1:T(8,128)(2,1)} %param.13) | copy-start | bytes 884740
Sparse Core Ops, SparseCore 0:
  9.0 186.8 all-gather.6
  197.6 380.8 all-gather.8
  601.1 111.1 all-gather.10
  713.8 110.4 all-gather.12
